TPU v7x, 32 devices: a whole 2x2x4 slice. The times are simulated.
32 devices in a mesh: shot: 4 (over y, core), tile: 8 (over z, x).
Axes of the slice: x: 2, y: 2, z: 4, core: 2. Of those that a mesh axis runs over, the one named last changes fastest.
Arguments:
- coefs: float32 [3, 16, 1024, 128], P(None, 'shot', 'tile')
- fwd_state: float32 [4, 4, 16, 1024, 128], P('shot', None, None, 'tile'), may hold values from -3 to 3
- adj_state: float32 [4, 4, 16, 1024, 128], P('shot', None, None, 'tile'), may hold values from -3 to 3
- src_cell: int32 [4, 8], P('shot', 'tile'), may hold values from 0 to 262143
- src_wave: float32 [4, 6], P('shot'), may hold values from -8 to 8
- rec_cells: int32 [4, 1024], P('shot', 'tile'), may hold values from 0 to 262143
- observed: float32 [4, 6, 1024], P('shot', None, 'tile'), may hold values from -6 to 6
Outputs:
- gradient: float32 [3, 16, 1024, 128], P(None, 'shot', 'tile')
- fwd_final: float32 [4, 2, 16, 1024, 128], P('shot', None, None, 'tile')
- adj_final: float32 [4, 2, 16, 1024, 128], P('shot', None, None, 'tile')
Inputs may be any that keep to these rules, and one draw needn't show every extreme that they name: `src_cell`: local cell index depth * 128 * 128 + first * 128 + second inside the aperture tile. `rec_cells`: local cell index inside the tile of the receiver's block; cells may repeat.
All inputs are finite; a program needn't handle non-finite values.
Results may differ from a plain program's by a relative error of at most 0.0003.
Values sent between devices are 32-bit elements; how exact they have to be, the bound alone decides.
No kernel may reach another device: no remote copies, remote signals or barrier semaphores. Data moves between devices by JAX's collectives and lax.ppermute only.
A program may use at most 192 MiB of HBM per device.

v0:
```python
import jax
import jax.numpy as jnp
from jax import lax
from jax.sharding import PartitionSpec as P

HALO = 12


def taps(padded, size, axis):

    def part(k):
        return lax.slice_in_dim(padded, k, k + size, axis=axis)

    return (-part(0) + 16.0 * part(1) - 30.0 * part(2) + 16.0 * part(3) - part(4)) / 12.0


def along_local(field, axis):
    pads = [(0, 0)] * field.ndim
    pads[axis] = (2, 2)
    return taps(jnp.pad(field, pads), field.shape[axis], axis)


def horiz(field):
    return along_local(field, field.ndim - 2) + along_local(field, field.ndim - 1)


def to_left_right(head, tail, axis):
    count = lax.axis_size(axis)
    from_left = lax.ppermute(tail, axis, [(i, i + 1) for i in range(count - 1)])
    from_right = lax.ppermute(head, axis, [(i + 1, i) for i in range(count - 1)])
    return (from_left, from_right)


def rows(x):
    return x.reshape(-1, x.shape[-1])


def per_device(coefs, fwd_state, adj_state, src_cell, src_wave, rec_cells, observed):
    w = HALO
    _, zl, ax, ay = coefs.shape
    n_tile = lax.axis_size("tile")
    tile = lax.axis_index("tile")
    steps = src_wave.shape[1]
    full = lax.all_gather(coefs, "shot", axis=1, tiled=True)
    az = full.shape[1]
    xe = ax + 2 * w
    ext_shape = (az, xe, ay)
    cells_ext = az * xe * ay
    fs = fwd_state[0]
    src_row = jnp.broadcast_to(src_cell[0, 0].astype(jnp.float32), (1, ay))
    head1 = jnp.concatenate([rows(fs[:, :, :w]), rows(coefs[:, :, :w]), src_row], axis=0)
    tail1 = jnp.concatenate(
        [rows(fs[:, :, ax - w :]), rows(coefs[:, :, ax - w :]), src_row], axis=0
    )
    left1, right1 = to_left_right(head1, tail1, "tile")
    n_fs = 4 * az * w
    n_cf = 3 * zl * w

    def unpack1(m):
        st = m[:n_fs].reshape(4, az, w, ay)
        cf = m[n_fs : n_fs + n_cf].reshape(3, zl, w, ay)
        sc = m[n_fs + n_cf, 0]
        return (st, cf, sc)

    st_l, cf_l, sc_l = unpack1(left1)
    st_r, cf_r, sc_r = unpack1(right1)
    cf_halo = lax.all_gather(jnp.concatenate([cf_l, cf_r], axis=2), "shot", axis=1, tiled=True)
    full_ext = jnp.concatenate([cf_halo[:, :, :w], full, cf_halo[:, :, w:]], axis=2)
    speed, stretch, couple = (full_ext[0], full_ext[1], full_ext[2])
    state = jnp.concatenate([st_l, fs, st_r], axis=2)
    ad = adj_state[0]
    left2, right2 = to_left_right(rows(ad[:, :, :w]), rows(ad[:, :, ax - w :]), "tile")
    adj_ext = jnp.concatenate(
        [left2.reshape(4, az, w, ay), ad, right2.reshape(4, az, w, ay)], axis=2
    )

    def ext_index(cell, shift):
        depth = cell // (ax * ay)
        first = cell // ay % ax + shift + w
        second = cell % ay
        ok = (first >= 0) & (first < xe)
        return (jnp.where(ok, (depth * xe + first) * ay + second, cells_ext), ok)

    src_own, _ = ext_index(src_cell[0, 0], 0)
    src_lft, ok_l = ext_index(sc_l.astype(jnp.int32), -ax)
    src_rgt, ok_r = ext_index(sc_r.astype(jnp.int32), ax)
    ok_l = ok_l & (tile > 0)
    ok_r = ok_r & (tile < n_tile - 1)
    src_idx = jnp.stack([src_own, src_lft, src_rgt])
    src_on = jnp.stack([jnp.float32(1.0), ok_l.astype(jnp.float32), ok_r.astype(jnp.float32)])
    source_mask = (
        jnp.zeros((cells_ext,), jnp.float32).at[src_idx].add(src_on, mode="drop").reshape(ext_shape)
    )
    receivers = rec_cells[0]
    rec_own, _ = ext_index(receivers, 0)
    upper, lower, upper_old, lower_old = (state[0], state[1], state[2], state[3])
    stored = []
    records = []
    for step in range(steps):
        h = horiz(upper)
        z = along_local(lower, 0)
        pulse = src_wave[0, step] * source_mask
        upper_next = 2.0 * upper - upper_old + speed * (stretch * h + couple * z) + pulse
        lower_next = 2.0 * lower - lower_old + speed * (couple * h + z) + pulse
        stored.append((h[:, w : w + ax], z[:, w : w + ax]))
        records.append(upper_next.reshape(-1)[rec_own] - observed[0, step])
        upper_old, lower_old, upper, lower = (upper, lower, upper_next, lower_next)
    msg = jnp.concatenate([jnp.stack(records), receivers.astype(jnp.float32)[None]], axis=0)
    left3, right3 = to_left_right(msg, msg, "tile")
    rec_l, okr_l = ext_index(left3[steps].astype(jnp.int32), -ax)
    rec_r, okr_r = ext_index(right3[steps].astype(jnp.int32), ax)
    okr_l = okr_l & (tile > 0)
    okr_r = okr_r & (tile < n_tile - 1)
    rec_l = jnp.where(okr_l, rec_l, cells_ext)
    rec_r = jnp.where(okr_r, rec_r, cells_ext)
    rec_all = jnp.concatenate([rec_own, rec_l, rec_r])
    lam, mu, lam_old, mu_old = (adj_ext[0], adj_ext[1], adj_ext[2], adj_ext[3])
    acc_h = jnp.zeros((az, ax, ay), jnp.float32)
    acc_x = jnp.zeros((az, ax, ay), jnp.float32)
    acc_z = jnp.zeros((az, ax, ay), jnp.float32)
    for step in reversed(range(steps)):
        first = speed * (stretch * lam + couple * mu)
        other = speed * (couple * lam + mu)
        vals = jnp.concatenate([records[step], left3[step], right3[step]])
        inject = (
            jnp.zeros((cells_ext,), jnp.float32)
            .at[rec_all]
            .add(vals, mode="drop")
            .reshape(ext_shape)
        )
        lam_new = inject + 2.0 * lam + horiz(first) - lam_old
        mu_new = 2.0 * mu + along_local(other, 0) - mu_old
        h, z = stored[step]
        ln = lam_new[:, w : w + ax]
        mn = mu_new[:, w : w + ax]
        acc_h = acc_h + ln * h
        acc_x = acc_x + ln * z + mn * h
        acc_z = acc_z + mn * z
        lam_old, mu_old, lam, mu = (lam, mu, lam_new, mu_new)
    n_shot = lax.axis_size("shot")
    acc = jnp.stack([acc_h, acc_x, acc_z])
    acc = acc.reshape(3, n_shot, az // n_shot, ax, ay).transpose(1, 0, 2, 3, 4)
    summed = lax.psum_scatter(acc, "shot", scatter_dimension=0, tiled=True)[0]
    q_h, q_x, q_z = (summed[0], summed[1], summed[2])
    c, a, b = (coefs[0], coefs[1], coefs[2])
    gradient = jnp.stack([a * q_h + b * q_x + q_z, c * q_h, c * q_x])
    fwd_final = jnp.stack([upper[:, w : w + ax], lower[:, w : w + ax]])[None]
    adj_final = jnp.stack([lam[:, w : w + ax], mu[:, w : w + ax]])[None]
    return (gradient, fwd_final, adj_final)


def solution(mesh):
    placed = (
        P(None, "shot", "tile", None),
        P("shot", None, None, "tile", None),
        P("shot", None, None, "tile", None),
        P("shot", "tile"),
        P("shot", None),
        P("shot", "tile"),
        P("shot", None, "tile"),
    )
    return jax.shard_map(
        per_device,
        mesh=mesh,
        in_specs=placed,
        out_specs=(
            P(None, "shot", "tile", None),
            P("shot", None, None, "tile", None),
            P("shot", None, None, "tile", None),
        ),
        check_vma=False,
    )
```

profile of v0, /device:TPU:0, one launch (start us, length us, event | category | flops | bytes accessed | tf_op | source)
XLA Modules:
  0.0 317.3 jit_solution(9708239038787714301)
XLA Ops:
  12.6 5.5 %collective-permute-start = (f32[913,128]{1,0:T(8,128)S(1)}, f32[913,128]{1,0:T(8,128)S(1)}, u32[]{:S(2)}, u32[]{:S(2)}) collective-permute-start(f32[913,128]{1,0:T(8,128)S(1)} %get-tuple-element.91), channel_id=1, source_target_pairs={{0,1},{1,2},{2,3},{3,4},{4,5},{5,6},{6,7},{8,9},{9,10},{10,11},{11... | collective-permute-start | bytes 1402376 | tf_op jit(solution)/shard_map/ppermute | solution.py:29
  21.6 6.2 %collective-permute-start.4 = (f32[768,128]{1,0:T(8,128)}, f32[768,128]{1,0:T(8,128)}, u32[]{:S(2)}, u32[]{:S(2)}) collective-permute-start(f32[768,128]{1,0:T(8,128)} %reshape.631), channel_id=1, source_target_pairs={{0,1},{1,2},{2,3},{3,4},{4,5},{5,6},{6,7},{8,9},{9,10},{10,11},{11... | collective-permute-start | bytes 1179656 | tf_op jit(solution)/shard_map/ppermute | solution.py:29
  28.7 6.7 %collective-permute-done.5 = f32[768,128]{1,0:T(8,128)S(1)} collective-permute-done((f32[768,128]{1,0:T(8,128)S(1)}, f32[768,128]{1,0:T(8,128)S(1)}, u32[]{:S(2)}, u32[]{:S(2)}) %collective-permute-start.5) | collective-permute-done | bytes 393248 | tf_op jit(solution)/shard_map/ppermute | solution.py:30
  35.4 18.7 %collective-permute-done.4 = f32[768,128]{1,0:T(8,128)} collective-permute-done((f32[768,128]{1,0:T(8,128)}, f32[768,128]{1,0:T(8,128)}, u32[]{:S(2)}, u32[]{:S(2)}) %collective-permute-start.4) | collective-permute-done | bytes 393248 | tf_op jit(solution)/shard_map/ppermute | solution.py:29
  57.9 7.6 %all_gather.6 = f32[3,16,24,128]{3,2,1,0:T(8,128)S(1)} all-gather(f32[3,4,24,128]{3,2,1,0:T(8,128)S(1)} %pad_maximum_fusion.4), channel_id=1, replica_groups=mesh['shot'=4,'tile'=8] {'shot'}, dimensions={1}, use_global_device_ids=true | all-gather | bytes 737280 | tf_op jit(solution)/shard_map/all_gather | solution.py:67
  67.6 5.5 %pad_maximum_fusion = (f32[4,16,152,128]{3,2,1,0:T(8,128)S(1)}, f32[4,16,152,128]{3,2,1,0:T(8,128)}) fusion(f32[4,16,12,128]{3,2,1,0:T(8,128)S(1)} %reshape.621, f32[4,16,128,128]{3,2,1,0:T(8,128)} %bitcast.466, f32[4,16,12,128]{3,2,1,0:T(8,128)S(1)} %reshape.618, f32[4,16,12,128]{3,2,1,0:T(8,128)S(1)} %reshape.634, f32[4,16,128,128]{3,2,1,0:T(8,128)} %bitcast.468, ...), kind=kLoop, calls=%fused_computation.13 | loop fusion | flops 4980736 | bytes 19922944 | tf_op jit(solution)/shard_map/concatenate | solution.py:70
  73.1 1.7 slice_bitcast_fusion.5
  76.3 2.2 scatter_custom_fusion
  78.5 7.6 %broadcast_multiply_fusion = (f32[311296]{0:T(1024)}, f32[311296]{0:T(1024)}, f32[311296]{0:T(1024)}, f32[311296]{0:T(1024)}, f32[311296]{0:T(1024)S(1)}, /*index=5*/f32[311296]{0:T(1024)S(1)}) fusion(f32[311296]{0:T(1024)} %scatter_custom_fusion, f32[]{:T(128)} %bitcast.46, f32[]{:T(128)} %bitcast.41, f32[]{:T(128)} %bitcast.36, f32[]{:T(128)} %bitcast.31, ...), kind=kLoop, calls=%fused_computation.422 | loop fusion | flops 1867776 | bytes 8716312 | tf_op jit(solution)/shard_map/mul | solution.py:102
  86.1 2.7 pad_maximum_fusion.2
  93.1 5.0 %add_multiply_fusion.10 = (f32[16,152,128]{2,1,0:T(8,128)}, f32[16,152,128]{2,1,0:T(8,128)}, f32[16,152,128]{2,1,0:T(8,128)S(1)}, f32[16,152,128]{2,1,0:T(8,128)S(1)}, f32[16,152,128]{2,1,0:T(8,128)S(1)}) fusion(f32[4,16,152,128]{3,2,1,0:T(8,128)} %get-tuple-element.112, f32[3,16,152,128]{3,2,1,0:T(8,128)S(1)} %pad_maximum_fusion.2, ...), kind=kLoop, calls=%fused_computation.367 | loop fusion | flops 12451840 | bytes 18677760 | tf_op jit(solution)/shard_map/mul | solution.py:123
  99.6 2.3 add_add_fusion.7
  102.5 1.6 copy-done.2
  104.1 3.0 add_add_fusion.5
  108.5 6.6 %add_add_fusion.3 = (f32[16,152,128]{2,1,0:T(8,128)}, f32[16,152,128]{2,1,0:T(8,128)}, f32[16,152,128]{2,1,0:T(8,128)}) fusion(f32[16,152,128]{2,1,0:T(8,128)S(1)} %bitcast.451, f32[16,152,128]{2,1,0:T(8,128)S(1)} %get-tuple-element.36, f32[16,152,128]{2,1,0:T(8,128)S(1)} %bitcast.433, f32[16,152,128]{2,1,0:T(8,128)S(1)} %get-tuple-element.35, ...), kind=kLoop, calls=%fused_computation.376 | loop fusion | flops 12451840 | bytes 16187392 | tf_op jit(solution)/shard_map/add | solution.py:104
  115.0 4.4 %add_add_fusion.4 = f32[16,152,128]{2,1,0:T(8,128)} fusion(f32[16,152,128]{2,1,0:T(8,128)} %bitcast.447, f32[16,152,128]{2,1,0:T(8,128)} %get-tuple-element.32, f32[16,152,128]{2,1,0:T(8,128)} %get-tuple-element.31, f32[3,16,152,128]{3,2,1,0:T(8,128)S(1)} %pad_maximum_fusion.2, f32[16,152,128]{2,1,0:T(8,128)S(1)} %bitcast.434, ...), kind=kLoop, calls=%fused_computation.379 | loop fusion | flops 7471104 | bytes 18677760 | tf_op jit(solution)/shard_map/add | solution.py:103
  119.4 12.8 %add_add_fusion.1 = (f32[16,152,128]{2,1,0:T(8,128)}, f32[16,152,128]{2,1,0:T(8,128)}, f32[16,152,128]{2,1,0:T(8,128)}) fusion(f32[16,152,128]{2,1,0:T(8,128)} %bitcast.452, f32[16,152,128]{2,1,0:T(8,128)} %bitcast.448, f32[16,152,128]{2,1,0:T(8,128)} %get-tuple-element.32, f32[16,152,128]{2,1,0:T(8,128)} %get-tuple-element.31, ...), kind=kLoop, calls=%fused_computation.372 | loop fusion | flops 14630912 | bytes 19922944 | tf_op jit(solution)/shard_map/add | solution.py:104
  132.2 6.8 %add_add_fusion.2 = f32[16,152,128]{2,1,0:T(8,128)} fusion(f32[16,152,128]{2,1,0:T(8,128)} %bitcast.453, f32[16,152,128]{2,1,0:T(8,128)} %get-tuple-element.29, f32[16,152,128]{2,1,0:T(8,128)} %get-tuple-element.28, f32[3,16,152,128]{3,2,1,0:T(8,128)S(1)} %pad_maximum_fusion.2, f32[16,152,128]{2,1,0:T(8,128)} %bitcast.449, ...), kind=kLoop, calls=%fused_computation.375 | loop fusion | flops 9961472 | bytes 22413312 | tf_op jit(solution)/shard_map/add | solution.py:103
  139.0 16.0 %add_add_fusion = (f32[16,152,128]{2,1,0:T(8,128)}, f32[16,152,128]{2,1,0:T(8,128)}, f32[16,152,128]{2,1,0:T(8,128)}) fusion(f32[16,152,128]{2,1,0:T(8,128)} %bitcast.457, f32[16,152,128]{2,1,0:T(8,128)} %bitcast.454, f32[16,152,128]{2,1,0:T(8,128)} %get-tuple-element.29, f32[16,152,128]{2,1,0:T(8,128)} %get-tuple-element.28, ...), kind=kLoop, calls=%fused_computation.371 | loop fusion | flops 20545536 | bytes 28639232 | tf_op jit(solution)/shard_map/add | solution.py:103
  155.0 2.1 gather_fusion.5
  157.2 2.0 gather_fusion.3
  159.2 2.0 gather_fusion.2
  161.1 2.0 gather_fusion.1
  163.1 2.0 gather_fusion
  165.1 2.0 gather_fusion.4
  168.5 5.0 %collective-permute-start.2 = (f32[7,128]{1,0:T(8,128)S(1)}, f32[7,128]{1,0:T(8,128)S(1)}, u32[]{:S(2)}, u32[]{:S(2)}) collective-permute-start(f32[7,128]{1,0:T(8,128)S(1)} %concatenate.93), channel_id=1, source_target_pairs={{0,1},{1,2},{2,3},{3,4},{4,5},{5,6},{6,7},{8,9},{9,10},{10,11},{11... | collective-permute-start | bytes 10760 | tf_op jit(solution)/shard_map/ppermute | solution.py:29
  174.9 4.4 %scatter_custom_fusion.1 = f32[311296]{0:T(1024)} fusion(s32[384]{0:T(512)S(1)} %fusion.260, f32[384]{0:T(512)S(1)} %pad_maximum_fusion.5, f32[]{:T(128)} %constant.225.clone.1), kind=kCustom, calls=%fused_computation.439 | custom fusion | flops 384 | bytes 1245188 | tf_op jit(solution)/shard_map/scatter-add | solution.py:128
  179.3 4.3 %scatter_custom_fusion.2 = f32[311296]{0:T(1024)} fusion(s32[384]{0:T(512)S(1)} %fusion.260, f32[384]{0:T(512)S(1)} %pad_maximum_fusion.6, f32[]{:T(128)} %constant.225.clone.1), kind=kCustom, calls=%fused_computation.437 | custom fusion | flops 384 | bytes 1245188 | tf_op jit(solution)/shard_map/scatter-add | solution.py:128
  183.6 4.4 %scatter_custom_fusion.3 = f32[311296]{0:T(1024)} fusion(s32[384]{0:T(512)S(1)} %fusion.260, f32[384]{0:T(512)S(1)} %pad_maximum_fusion.7, f32[]{:T(128)} %constant.225.clone.1), kind=kCustom, calls=%fused_computation.435 | custom fusion | flops 384 | bytes 1245188 | tf_op jit(solution)/shard_map/scatter-add | solution.py:128
  188.0 4.4 %scatter_custom_fusion.4 = f32[311296]{0:T(1024)} fusion(s32[384]{0:T(512)S(1)} %fusion.260, f32[384]{0:T(512)S(1)} %pad_maximum_fusion.8, f32[]{:T(128)} %constant.225.clone.1), kind=kCustom, calls=%fused_computation.433 | custom fusion | flops 384 | bytes 1245188 | tf_op jit(solution)/shard_map/scatter-add | solution.py:128
  192.4 4.6 %scatter_custom_fusion.5 = f32[311296]{0:T(1024)} fusion(s32[384]{0:T(512)S(1)} %fusion.260, f32[384]{0:T(512)S(1)} %pad_maximum_fusion.9, f32[]{:T(128)} %constant.225.clone.1), kind=kCustom, calls=%fused_computation.431 | custom fusion | flops 384 | bytes 1245188 | tf_op jit(solution)/shard_map/scatter-add | solution.py:128
  197.0 11.9 %add_multiply_fusion.9 = (f32[16,152,128]{2,1,0:T(8,128)S(1)}, f32[16,152,128]{2,1,0:T(8,128)S(1)}, f32[16,152,128]{2,1,0:T(8,128)S(1)}) fusion(f32[3,16,152,128]{3,2,1,0:T(8,128)} %copy-done, f32[4,16,152,128]{3,2,1,0:T(8,128)} %get-tuple-element.112, f32[16,152,128]{2,1,0:T(8,128)} %get-tuple-element.43, f32[16,152,128]{2,1,0:T(8,128)} %bitcast.474, ...), kind=kLoop, calls=%fused_computation.366 | loop fusion | flops 11517952 | bytes 16187392 | tf_op jit(solution)/shard_map/mul | solution.py:122
  209.2 1.9 copy-done.49
  211.1 3.7 %add_multiply_fusion.7 = (f32[16,152,128]{2,1,0:T(8,128)S(1)}, f32[16,152,128]{2,1,0:T(8,128)S(1)}, f32[16,152,128]{2,1,0:T(8,128)S(1)}) fusion(f32[3,16,152,128]{3,2,1,0:T(8,128)S(1)} %copy-done.1, f32[4,16,152,128]{3,2,1,0:T(8,128)} %get-tuple-element.112, f32[16,152,128]{2,1,0:T(8,128)S(1)} %get-tuple-element.21, f32[16,152,128]{2,1,0:T(8,128)S(1)} %bitcast.473, ...), kind=kLoop, calls=%fused_computation.362 | loop fusion | flops 11517952 | bytes 16187392 | tf_op jit(solution)/shard_map/mul | solution.py:122
  215.1 1.9 copy-done.48
  217.0 2.4 add_multiply_fusion.5
  219.7 1.9 copy-done.47
  221.6 2.4 add_multiply_fusion.3
  226.2 3.4 %add_multiply_fusion.1 = (f32[16,152,128]{2,1,0:T(8,128)S(1)}, f32[16,152,128]{2,1,0:T(8,128)}, f32[16,152,128]{2,1,0:T(8,128)}) fusion(f32[3,16,152,128]{3,2,1,0:T(8,128)S(1)} %copy-done.1, f32[16,152,128]{2,1,0:T(8,128)S(1)} %get-tuple-element.16, f32[16,152,128]{2,1,0:T(8,128)S(1)} %get-tuple-element.12, f32[16,152,128]{2,1,0:T(8,128)S(1)} %bitcast.470, ...), kind=kLoop, calls=%fused_computation.350 | loop fusion | flops 11517952 | bytes 16187392 | tf_op jit(solution)/shard_map/mul | solution.py:122
  229.7 4.2 %add_subtract_fusion = (f32[16,152,128]{2,1,0:T(8,128)}, f32[16,152,128]{2,1,0:T(8,128)}, f32[16,152,128]{2,1,0:T(8,128)}, f32[16,152,128]{2,1,0:T(8,128)}, f32[16,152,128]{2,1,0:T(8,128)}, /*index=5*/f32[16,152,128]{2,1,0:T(8,128)}) fusion(f32[16,152,128]{2,1,0:T(8,128)S(1)} %get-tuple-element.7), kind=kLoop, calls=%fused_computation.349 | loop fusion | flops 3424256 | bytes 8716288 | tf_op jit(solution)/shard_map/sub | solution.py:14
  233.9 4.7 %scatter_custom_fusion.6 = f32[311296]{0:T(1024)} fusion(s32[384]{0:T(512)S(1)} %fusion.260, f32[384]{0:T(512)S(1)} %pad_maximum_fusion.10, f32[]{:T(128)} %constant.225.clone.1), kind=kCustom, calls=%fused_computation.429 | custom fusion | flops 384 | bytes 1245188 | tf_op jit(solution)/shard_map/scatter-add | solution.py:128
  238.7 3.9 %broadcast_multiply_fusion.6 = (f32[16,152,128]{2,1,0:T(8,128)}, f32[16,152,128]{2,1,0:T(8,128)S(1)}) fusion(f32[16,152,128]{2,1,0:T(8,128)} %get-tuple-element.9, f32[16,152,128]{2,1,0:T(8,128)} %get-tuple-element.8, f32[3,16,152,128]{3,2,1,0:T(8,128)} %copy-done), kind=kLoop, calls=%fused_computation.428 | loop fusion | flops 1245184 | bytes 7471104 | tf_op jit(solution)/shard_map/mul | solution.py:14
  242.5 2.0 fusion.99
  246.7 5.2 %multiply_add_fusion.2 = (f32[16,128,128]{2,1,0:T(8,128)}, f32[16,128,128]{2,1,0:T(8,128)S(1)}) fusion(f32[16,152,128]{2,1,0:T(8,128)S(1)} %copy-done.37, f32[16,152,128]{2,1,0:T(8,128)S(1)} %copy-done.7, f32[16,152,128]{2,1,0:T(8,128)S(1)} %get-tuple-element.34, f32[16,152,128]{2,1,0:T(8,128)S(1)} %copy-done.12, f32[16,152,128]{2,1,0:T(8,128)S(1)} %copy-done.25, ...), kind=kLoop, calls=%fused_computation.420 | loop fusion | flops 5505024 | bytes 20971520 | tf_op jit(solution)/shard_map/add | solution.py:136
  253.2 6.5 %multiply_add_fusion.1 = (f32[16,128,128]{2,1,0:T(8,128)}, f32[16,128,128]{2,1,0:T(8,128)}) fusion(f32[16,128,128]{2,1,0:T(8,128)S(1)} %get-tuple-element.4, f32[16,152,128]{2,1,0:T(8,128)S(1)} %copy-done.35, f32[16,152,128]{2,1,0:T(8,128)S(1)} %copy-done.5, f32[16,152,128]{2,1,0:T(8,128)S(1)} %get-tuple-element.35, f32[16,152,128]{2,1,0:T(8,128)S(1)} %copy-done.19, ...), kind=kLoop, calls=%fused_computation.419 | loop fusion | flops 8126464 | bytes 30408704 | tf_op jit(solution)/shard_map/add | solution.py:137
  259.8 5.0 %fusion.232 = (f32[1,16,128,128]{3,2,1,0:T(8,128)S(1)}, f32[16,128,128]{2,1,0:T(8,128)S(1)}) fusion(f32[16,152,128]{2,1,0:T(8,128)} %bitcast.458, f32[16,152,128]{2,1,0:T(8,128)} %get-tuple-element.51, f32[16,152,128]{2,1,0:T(8,128)} %get-tuple-element.30, f32[16,152,128]{2,1,0:T(8,128)} %get-tuple-element.27, f32[16,152,128]{2,1,0:T(8,128)} %get-tuple-element.50, ...), kind=kLoop, calls=%fused_computation.394 | loop fusion | flops 4718592 | bytes 20971520 | tf_op jit(solution)/shard_map/stack | solution.py:147
  264.8 2.0 maximum_bitcast_fusion
  271.3 36.7 %reduce-scatter.2.cloned.1.call-done = f32[1,3,4,128,128]{4,3,2,1,0:T(8,128)} async-done(((f32[4,3,4,128,128]{4,3,2,1,0:T(8,128)}), f32[1,3,4,128,128]{4,3,2,1,0:T(8,128)}) %reduce-scatter.2.cloned.1.call-update) | async-done | bytes 786448 | tf_op jit(solution)/shard_map/reduce_scatter | solution.py:143
  (190 shorter events, 37.9 us)
Async XLA Ops:
  7.2 79.0 %all-gather.2.cloned.1.call-start = ((), (), s32[]{:S(2)}) async-start(), calls=%async_computation.1 | async-start | bytes 3932160 | tf_op jit(solution)/shard_map/all_gather | solution.py:44
  7.9 300.1 %reduce-scatter.2.cloned.1.call-start = ((), (), s32[]{:S(2)}) async-start(), calls=%async_computation.2 | async-start | bytes 3932160 | tf_op jit(solution)/shard_map/reduce_scatter | solution.py:143
  11.3 43.9 %collective-permute-start.1 = (f32[913,128]{1,0:T(8,128)S(1)}, f32[913,128]{1,0:T(8,128)S(1)}, u32[]{:S(2)}, u32[]{:S(2)}) collective-permute-start(f32[913,128]{1,0:T(8,128)S(1)} %get-tuple-element.92), channel_id=1, source_target_pairs={{1,0},{2,1},{3,2},{4,3},{5,4},{6,5},{7,6},{9,8},{10,9},{11,10},{12... | collective-permute-start | bytes 1402376 | tf_op jit(solution)/shard_map/ppermute | solution.py:30
  12.6 43.9 %collective-permute-start = (f32[913,128]{1,0:T(8,128)S(1)}, f32[913,128]{1,0:T(8,128)S(1)}, u32[]{:S(2)}, u32[]{:S(2)}) collective-permute-start(f32[913,128]{1,0:T(8,128)S(1)} %get-tuple-element.91), channel_id=1, source_target_pairs={{0,1},{1,2},{2,3},{3,4},{4,5},{5,6},{6,7},{8,9},{9,10},{10,11},{11... | collective-permute-start | bytes 1402376 | tf_op jit(solution)/shard_map/ppermute | solution.py:29
  19.5 8.3 %copy-start.58 = (s32[1,128]{1,0:T(1,128)S(1)}, s32[1,128]{1,0:T(1,128)}, u32[]{:S(2)}) copy-start(s32[1,128]{1,0:T(1,128)} %param.12) | copy-start | bytes 1540
  19.5 8.5 %copy-start.56 = (f32[1,6]{1,0:T(1,128)S(1)}, f32[1,6]{1,0:T(1,128)}, u32[]{:S(2)}) copy-start(f32[1,6]{1,0:T(1,128)} %param.11) | copy-start | bytes 76
  19.6 15.8 %collective-permute-start.5 = (f32[768,128]{1,0:T(8,128)S(1)}, f32[768,128]{1,0:T(8,128)S(1)}, u32[]{:S(2)}, u32[]{:S(2)}) collective-permute-start(f32[768,128]{1,0:T(8,128)S(1)} %reshape.633), channel_id=1, source_target_pairs={{1,0},{2,1},{3,2},{4,3},{5,4},{6,5},{7,6},{9,8},{10,9},{11,10},{12... | collective-permute-start | bytes 1179656 | tf_op jit(solution)/shard_map/ppermute | solution.py:30
  21.6 32.5 %collective-permute-start.4 = (f32[768,128]{1,0:T(8,128)}, f32[768,128]{1,0:T(8,128)}, u32[]{:S(2)}, u32[]{:S(2)}) collective-permute-start(f32[768,128]{1,0:T(8,128)} %reshape.631), channel_id=1, source_target_pairs={{0,1},{1,2},{2,3},{3,4},{4,5},{5,6},{6,7},{8,9},{9,10},{10,11},{11... | collective-permute-start | bytes 1179656 | tf_op jit(solution)/shard_map/ppermute | solution.py:29
  86.1 15.7 %copy-start.9 = (f32[311296]{0:T(1024)}, f32[311296]{0:T(1024)S(1)}, u32[]{:S(2)}) copy-start(f32[311296]{0:T(1024)S(1)} %get-tuple-element.73) | copy-start | bytes 3735556
  86.1 4.3 %slice-start = ((s8[4980736]{0:T(1024)(128)(4,1)}), s8[4194304]{0:T(1024)(128)(4,1)S(1)}, s32[]{:S(2)}) async-start(s8[4980736]{0:T(1024)(128)(4,1)} %bitcast.438), calls=%async_computation.3 | async-start | bytes 8388608
  86.1 4.3 %slice-start.1 = ((s8[4980736]{0:T(1024)(128)(4,1)}), s8[786432]{0:T(1024)(128)(4,1)S(1)}, s32[]{:S(2)}) async-start(s8[4980736]{0:T(1024)(128)(4,1)} %bitcast.438), calls=%async_computation.4 | async-start | bytes 1572864
  88.8 50.2 %copy-start = (f32[3,16,152,128]{3,2,1,0:T(8,128)}, f32[3,16,152,128]{3,2,1,0:T(8,128)S(1)}, u32[]{:S(2)}) copy-start(f32[3,16,152,128]{3,2,1,0:T(8,128)S(1)} %pad_maximum_fusion.2) | copy-start | bytes 11206660
  88.8 4.3 %copy-start.45 = (f32[16,152,128]{2,1,0:T(8,128)S(1)}, f32[16,152,128]{2,1,0:T(8,128)}, u32[]{:S(2)}) copy-start(f32[16,152,128]{2,1,0:T(8,128)} %get-tuple-element.45) | copy-start | bytes 3735556
  98.1 10.0 %copy-start.26 = (f32[16,152,128]{2,1,0:T(8,128)}, f32[16,152,128]{2,1,0:T(8,128)S(1)}, u32[]{:S(2)}) copy-start(f32[16,152,128]{2,1,0:T(8,128)S(1)} %get-tuple-element.52) | copy-start | bytes 3735556
  99.6 15.5 %copy-start.8 = (f32[16,152,128]{2,1,0:T(8,128)}, f32[16,152,128]{2,1,0:T(8,128)S(1)}, u32[]{:S(2)}) copy-start(f32[16,152,128]{2,1,0:T(8,128)S(1)} %fusion.220) | copy-start | bytes 3735556
  101.8 6.3 %copy-start.33 = (f32[16,152,128]{2,1,0:T(8,128)}, f32[16,152,128]{2,1,0:T(8,128)S(1)}, u32[]{:S(2)}) copy-start(f32[16,152,128]{2,1,0:T(8,128)S(1)} %get-tuple-element.36) | copy-start | bytes 3735556
  101.9 37.2 %copy-start.4 = (f32[16,152,128]{2,1,0:T(8,128)}, f32[16,152,128]{2,1,0:T(8,128)S(1)}, u32[]{:S(2)}) copy-start(f32[16,152,128]{2,1,0:T(8,128)S(1)} %get-tuple-element.38) | copy-start | bytes 3735556
  101.9 37.2 %copy-start.6 = (f32[16,152,128]{2,1,0:T(8,128)}, f32[16,152,128]{2,1,0:T(8,128)S(1)}, u32[]{:S(2)}) copy-start(f32[16,152,128]{2,1,0:T(8,128)S(1)} %get-tuple-element.37) | copy-start | bytes 3735556
  102.5 4.7 %copy-start.42 = (f32[16,152,128]{2,1,0:T(8,128)}, f32[16,152,128]{2,1,0:T(8,128)S(1)}, u32[]{:S(2)}) copy-start(f32[16,152,128]{2,1,0:T(8,128)S(1)} %add_add_fusion.8) | copy-start | bytes 3735556
  108.1 6.9 %copy-start.41 = (f32[16,152,128]{2,1,0:T(8,128)}, f32[16,152,128]{2,1,0:T(8,128)S(1)}, u32[]{:S(2)}) copy-start(f32[16,152,128]{2,1,0:T(8,128)S(1)} %add_add_fusion.6) | copy-start | bytes 3735556
  157.2 10.0 %copy-start.57 = (f32[1,6,128]{2,0,1:T(1,128)S(1)}, f32[1,6,128]{2,0,1:T(1,128)}, u32[]{:S(2)}) copy-start(f32[1,6,128]{2,0,1:T(1,128)} %param.13) | copy-start | bytes 9220
  167.2 6.3 %collective-permute-start.3 = (f32[7,128]{1,0:T(8,128)S(1)}, f32[7,128]{1,0:T(8,128)S(1)}, u32[]{:S(2)}, u32[]{:S(2)}) collective-permute-start(f32[7,128]{1,0:T(8,128)S(1)} %concatenate.93), channel_id=1, source_target_pairs={{1,0},{2,1},{3,2},{4,3},{5,4},{6,5},{7,6},{9,8},{10,9},{11,10},{12... | collective-permute-start | bytes 10760 | tf_op jit(solution)/shard_map/ppermute | solution.py:30
  168.5 6.3 %collective-permute-start.2 = (f32[7,128]{1,0:T(8,128)S(1)}, f32[7,128]{1,0:T(8,128)S(1)}, u32[]{:S(2)}, u32[]{:S(2)}) collective-permute-start(f32[7,128]{1,0:T(8,128)S(1)} %concatenate.93), channel_id=1, source_target_pairs={{0,1},{1,2},{2,3},{3,4},{4,5},{5,6},{6,7},{8,9},{9,10},{10,11},{11... | collective-permute-start | bytes 10760 | tf_op jit(solution)/shard_map/ppermute | solution.py:29
  197.0 11.9 %copy-start.1 = (f32[3,16,152,128]{3,2,1,0:T(8,128)S(1)}, f32[3,16,152,128]{3,2,1,0:T(8,128)}, u32[]{:S(2)}) copy-start(f32[3,16,152,128]{3,2,1,0:T(8,128)} %copy-done) | copy-start | bytes 11206660
  208.9 6.2 %copy-start.14 = (f32[16,152,128]{2,1,0:T(8,128)}, f32[16,152,128]{2,1,0:T(8,128)S(1)}, u32[]{:S(2)}) copy-start(f32[16,152,128]{2,1,0:T(8,128)S(1)} %get-tuple-element.23) | copy-start | bytes 3735556
  208.9 6.2 %copy-start.20 = (f32[16,152,128]{2,1,0:T(8,128)}, f32[16,152,128]{2,1,0:T(8,128)S(1)}, u32[]{:S(2)}) copy-start(f32[16,152,128]{2,1,0:T(8,128)S(1)} %get-tuple-element.22) | copy-start | bytes 3735556
  214.8 4.9 %copy-start.16 = (f32[16,152,128]{2,1,0:T(8,128)}, f32[16,152,128]{2,1,0:T(8,128)S(1)}, u32[]{:S(2)}) copy-start(f32[16,152,128]{2,1,0:T(8,128)S(1)} %get-tuple-element.20) | copy-start | bytes 3735556
  214.8 4.9 %copy-start.22 = (f32[16,152,128]{2,1,0:T(8,128)}, f32[16,152,128]{2,1,0:T(8,128)S(1)}, u32[]{:S(2)}) copy-start(f32[16,152,128]{2,1,0:T(8,128)S(1)} %get-tuple-element.19) | copy-start | bytes 3735556
  219.4 4.9 %copy-start.18 = (f32[16,152,128]{2,1,0:T(8,128)}, f32[16,152,128]{2,1,0:T(8,128)S(1)}, u32[]{:S(2)}) copy-start(f32[16,152,128]{2,1,0:T(8,128)S(1)} %get-tuple-element.17) | copy-start | bytes 3735556
  219.4 4.9 %copy-start.24 = (f32[16,152,128]{2,1,0:T(8,128)}, f32[16,152,128]{2,1,0:T(8,128)S(1)}, u32[]{:S(2)}) copy-start(f32[16,152,128]{2,1,0:T(8,128)S(1)} %get-tuple-element.16) | copy-start | bytes 3735556
  238.6 5.9 %copy-start.25 = (f32[16,152,128]{2,1,0:T(8,128)S(1)}, f32[16,152,128]{2,1,0:T(8,128)}, u32[]{:S(2)}) copy-start(f32[16,152,128]{2,1,0:T(8,128)} %copy-done.24) | copy-start | bytes 3735556
  238.6 5.9 %copy-start.28 = (f32[16,152,128]{2,1,0:T(8,128)S(1)}, f32[16,152,128]{2,1,0:T(8,128)}, u32[]{:S(2)}) copy-start(f32[16,152,128]{2,1,0:T(8,128)} %get-tuple-element.28) | copy-start | bytes 3735556
  238.6 5.9 %copy-start.32 = (f32[16,152,128]{2,1,0:T(8,128)S(1)}, f32[16,152,128]{2,1,0:T(8,128)}, u32[]{:S(2)}) copy-start(f32[16,152,128]{2,1,0:T(8,128)} %copy-done.31) | copy-start | bytes 3735556
  238.6 5.9 %copy-start.37 = (f32[16,152,128]{2,1,0:T(8,128)S(1)}, f32[16,152,128]{2,1,0:T(8,128)}, u32[]{:S(2)}) copy-start(f32[16,152,128]{2,1,0:T(8,128)} %copy-done.36) | copy-start | bytes 3735556
  238.7 5.9 %copy-start.38 = (f32[16,152,128]{2,1,0:T(8,128)S(1)}, f32[16,152,128]{2,1,0:T(8,128)}, u32[]{:S(2)}) copy-start(f32[16,152,128]{2,1,0:T(8,128)} %get-tuple-element.8) | copy-start | bytes 3735556
  238.7 5.9 %copy-start.39 = (f32[16,152,128]{2,1,0:T(8,128)S(1)}, f32[16,152,128]{2,1,0:T(8,128)}, u32[]{:S(2)}) copy-start(f32[16,152,128]{2,1,0:T(8,128)} %get-tuple-element.25) | copy-start | bytes 3735556
  242.5 4.1 %copy-start.23 = (f32[16,152,128]{2,1,0:T(8,128)S(1)}, f32[16,152,128]{2,1,0:T(8,128)}, u32[]{:S(2)}) copy-start(f32[16,152,128]{2,1,0:T(8,128)} %copy-done.22) | copy-start | bytes 3735556
  246.7 5.3 %copy-start.5 = (f32[16,152,128]{2,1,0:T(8,128)S(1)}, f32[16,152,128]{2,1,0:T(8,128)}, u32[]{:S(2)}) copy-start(f32[16,152,128]{2,1,0:T(8,128)} %copy-done.4) | copy-start | bytes 3735556
  246.7 5.3 %copy-start.11 = (f32[16,152,128]{2,1,0:T(8,128)S(1)}, f32[16,152,128]{2,1,0:T(8,128)}, u32[]{:S(2)}) copy-start(f32[16,152,128]{2,1,0:T(8,128)} %get-tuple-element.32) | copy-start | bytes 3735556
  246.7 5.3 %copy-start.15 = (f32[16,152,128]{2,1,0:T(8,128)S(1)}, f32[16,152,128]{2,1,0:T(8,128)}, u32[]{:S(2)}) copy-start(f32[16,152,128]{2,1,0:T(8,128)} %copy-done.14) | copy-start | bytes 3735556
  246.7 5.3 %copy-start.17 = (f32[16,152,128]{2,1,0:T(8,128)S(1)}, f32[16,152,128]{2,1,0:T(8,128)}, u32[]{:S(2)}) copy-start(f32[16,152,128]{2,1,0:T(8,128)} %copy-done.16) | copy-start | bytes 3735556
  246.7 5.3 %copy-start.19 = (f32[16,152,128]{2,1,0:T(8,128)S(1)}, f32[16,152,128]{2,1,0:T(8,128)}, u32[]{:S(2)}) copy-start(f32[16,152,128]{2,1,0:T(8,128)} %copy-done.18) | copy-start | bytes 3735556
  246.7 5.8 %copy-start.27 = (f32[16,152,128]{2,1,0:T(8,128)S(1)}, f32[16,152,128]{2,1,0:T(8,128)}, u32[]{:S(2)}) copy-start(f32[16,152,128]{2,1,0:T(8,128)} %get-tuple-element.29) | copy-start | bytes 3735556
  246.7 6.2 %copy-start.30 = (f32[16,152,128]{2,1,0:T(8,128)S(1)}, f32[16,152,128]{2,1,0:T(8,128)}, u32[]{:S(2)}) copy-start(f32[16,152,128]{2,1,0:T(8,128)} %copy-done.29) | copy-start | bytes 3735556
  246.7 6.5 %copy-start.35 = (f32[16,152,128]{2,1,0:T(8,128)S(1)}, f32[16,152,128]{2,1,0:T(8,128)}, u32[]{:S(2)}) copy-start(f32[16,152,128]{2,1,0:T(8,128)} %copy-done.34) | copy-start | bytes 3735556
  259.8 5.1 %copy-start.50 = (f32[16,128,128]{2,1,0:T(8,128)S(1)}, f32[16,128,128]{2,1,0:T(8,128)}, u32[]{:S(2)}) copy-start(f32[16,128,128]{2,1,0:T(8,128)} %get-tuple-element.3) | copy-start | bytes 3145732
  259.8 5.1 %copy-start.51 = (f32[16,128,128]{2,1,0:T(8,128)S(1)}, f32[16,128,128]{2,1,0:T(8,128)}, u32[]{:S(2)}) copy-start(f32[16,128,128]{2,1,0:T(8,128)} %get-tuple-element.5) | copy-start | bytes 3145732
  269.8 38.2 %copy-start.52 = (f32[3,4,128,128]{3,2,1,0:T(8,128)S(1)}, f32[3,4,128,128]{3,2,1,0:T(8,128)}, u32[]{:S(2)}) copy-start(f32[3,4,128,128]{3,2,1,0:T(8,128)} %param.7) | copy-start | bytes 2359300
  (21 other events, 44.6 us)
Sparse Core Ops, SparseCore 0:
  9.5 31.2 all-gather.1
  267.0 40.9 reduce-scatter.1
where the time goes:
time: 322 us; the launch traced here: 317 us
  other arithmetic  163 us (51%)
  waiting for transfers between devices  64.1 us (20%)
  local copies, waits for them, and re-layouts  44.4 us (14%)
  starting transfers between devices  20.7 us (6%)
  between operations  17.5 us (5%)
  blocking collectives  7.56 us (2%)
    reduce_scatter x1, waiting for transfers between devices, per_device(): summed = lax.psum_scatter(acc, 'shot', scatter_dimension=0, tiled=True)[0]  36.7 us
    add x6, other arithmetic, per_device(): 2.0 * upper - upper_old + speed * (stretch * h + couple * z) + pulse  29.4 us
    scatter-add x6, other arithmetic, per_device(): inject = jnp.zeros((cells_ext,), jnp.float32).at[rec_all].add(vals, mode=...  26.7 us
    add x4, other arithmetic, per_device(): lower_next = 2.0 * lower - lower_old + speed * (couple * h + z) + pulse  24.6 us
    mul x5, other arithmetic, per_device(): first = speed * (stretch * lam + couple * mu)  23.8 us
    unnamed x122, local copies, waits for them, and re-layouts  20.3 us
    ppermute x3, waiting for transfers between devices, to_left_right(): from_left = lax.ppermute(tail, axis, [(i, i + 1) for i in range(count - 1)])  20 us
    ppermute x3, starting transfers between devices, to_left_right(): from_left = lax.ppermute(tail, axis, [(i, i + 1) for i in range(count - 1)])  16.7 us
  transfers between devices with their start and end apart: 8, of which 4 were waited for; matrix products, arithmetic and copies ran while one was open for 9% of the time, Pallas kernels for 0%

commit v1 on v0

--- a/solution.py
+++ b/solution.py
@@ -1,9 +1,32 @@
+import functools
 import jax
 import jax.numpy as jnp
 from jax import lax
 from jax.sharding import PartitionSpec as P
 
 HALO = 12
+
+
+def play_tracks_on(inner_x, where_dim):
+    inner_x = jnp.moveaxis(inner_x, 0, where_dim)
+    near = inner_x.shape
+    return inner_x.reshape(
+        *near[:where_dim], near[where_dim] * near[where_dim + 1], *near[where_dim + 2 :]
+    )
+
+
+def draft_face(point, link_axis, in_dim):
+    n = lax.axis_size(link_axis)
+    all_blocks = [(j0, (j0 + 1) % n) for j0 in range(n)]
+    panels = [point]
+    while len(panels) < n:
+        panels.append(lax.ppermute(panels[-1], link_axis, all_blocks))
+    block_now = lax.axis_index(link_axis)
+    panels = jnp.stack(panels)[(block_now - jnp.arange(n)) % n]
+    return play_tracks_on(panels, in_dim)
+
+
+_supply_state = functools.partial(draft_face, link_axis="shot", in_dim=1)
 
 
 def taps(padded, size, axis):
@@ -64,7 +87,7 @@
 
     st_l, cf_l, sc_l = unpack1(left1)
     st_r, cf_r, sc_r = unpack1(right1)
-    cf_halo = lax.all_gather(jnp.concatenate([cf_l, cf_r], axis=2), "shot", axis=1, tiled=True)
+    cf_halo = _supply_state(jnp.concatenate([cf_l, cf_r], axis=2))
     full_ext = jnp.concatenate([cf_halo[:, :, :w], full, cf_halo[:, :, w:]], axis=2)
     speed, stretch, couple = (full_ext[0], full_ext[1], full_ext[2])
     state = jnp.concatenate([st_l, fs, st_r], axis=2)

time: 322 us -> 327 us (1.016)
  local copies, waits for them, and re-layouts: 44.4 us -> 52.5 us
  blocking collectives: 7.56 us -> 0 us
    all_gather x1 -> x0, blocking collectives: 7.56 us -> none  [per_device(): lax.all_gather(jnp.concatenate([cf_l, cf_r], axis=2), 'shot', axis=1, til...]
    reshape x2, local copies, waits for them, and re-layouts: 0.07 us -> 3.65 us  [unpack1(): st = m[:n_fs].reshape(4, az, w, ay)]
    unnamed x122 -> x124, local copies, waits for them, and re-layouts: 20.3 us -> 18.3 us
  transfers between devices with their start and end apart: 8 -> 11, of which waited for: 4 -> 5; matrix products, arithmetic and copies ran while one was open for 9% -> 13% of each run, Pallas kernels for 0% -> 0%
where the time goes in v1:
time: 327 us; the launch traced here: 322 us
  other arithmetic  163 us (50%)
  waiting for transfers between devices  66.9 us (20%)
  local copies, waits for them, and re-layouts  52.5 us (16%)
  starting transfers between devices  22.1 us (7%)
  between operations  17.5 us (5%)
    reduce_scatter x1, waiting for transfers between devices, per_device(): summed = lax.psum_scatter(acc, 'shot', scatter_dimension=0, tiled=True)[0]  36 us
    add x6, other arithmetic, per_device(): 2.0 * upper - upper_old + speed * (stretch * h + couple * z) + pulse  29.2 us
    scatter-add x6, other arithmetic, per_device(): inject = jnp.zeros((cells_ext,), jnp.float32).at[rec_all].add(vals, mode=...  26.7 us
    add x4, other arithmetic, per_device(): lower_next = 2.0 * lower - lower_old + speed * (couple * h + z) + pulse  24.9 us
    mul x5, other arithmetic, per_device(): first = speed * (stretch * lam + couple * mu)  23.4 us
    ppermute x3, waiting for transfers between devices, to_left_right(): from_left = lax.ppermute(tail, axis, [(i, i + 1) for i in range(count - 1)])  19.9 us
    unnamed x124, local copies, waits for them, and re-layouts  18.3 us
    ppermute x3, starting transfers between devices, to_left_right(): from_left = lax.ppermute(tail, axis, [(i, i + 1) for i in range(count - 1)])  16 us
  transfers between devices with their start and end apart: 11, of which 5 were waited for; matrix products, arithmetic and copies ran while one was open for 13% of the time, Pallas kernels for 0%

profile of v1, /device:TPU:0, one launch (start us, length us, event | category | flops | bytes accessed | tf_op | source)
XLA Modules:
  0.0 322.5 jit_solution(4403478236334659430)
XLA Ops:
  12.6 6.3 %collective-permute-start = (f32[913,128]{1,0:T(8,128)S(1)}, f32[913,128]{1,0:T(8,128)}, u32[]{:S(2)}, u32[]{:S(2)}) collective-permute-start(f32[913,128]{1,0:T(8,128)S(1)} %get-tuple-element.91), channel_id=1, source_target_pairs={{0,1},{1,2},{2,3},{3,4},{4,5},{5,6},{6,7},{8,9},{9,10},{10,11},{11... | collective-permute-start | bytes 1402376 | tf_op jit(solution)/shard_map/ppermute | solution.py:52
  21.7 4.7 %collective-permute-start.7 = (f32[768,128]{1,0:T(8,128)S(1)}, f32[768,128]{1,0:T(8,128)S(1)}, u32[]{:S(2)}, u32[]{:S(2)}) collective-permute-start(f32[768,128]{1,0:T(8,128)S(1)} %reshape.684), channel_id=1, source_target_pairs={{0,1},{1,2},{2,3},{3,4},{4,5},{5,6},{6,7},{8,9},{9,10},{10,11},{11... | collective-permute-start | bytes 1179656 | tf_op jit(solution)/shard_map/ppermute | solution.py:52
  27.2 8.1 %collective-permute-done.8 = f32[768,128]{1,0:T(8,128)S(1)} collective-permute-done((f32[768,128]{1,0:T(8,128)S(1)}, f32[768,128]{1,0:T(8,128)S(1)}, u32[]{:S(2)}, u32[]{:S(2)}) %collective-permute-start.8) | collective-permute-done | bytes 393248 | tf_op jit(solution)/shard_map/ppermute | solution.py:53
  35.4 18.6 %collective-permute-done.7 = f32[768,128]{1,0:T(8,128)S(1)} collective-permute-done((f32[768,128]{1,0:T(8,128)S(1)}, f32[768,128]{1,0:T(8,128)S(1)}, u32[]{:S(2)}, u32[]{:S(2)}) %collective-permute-start.7) | collective-permute-done | bytes 393248 | tf_op jit(solution)/shard_map/ppermute | solution.py:52
  62.3 7.3 %broadcast_multiply_fusion = (f32[311296]{0:T(1024)}, f32[311296]{0:T(1024)}, f32[311296]{0:T(1024)}, f32[311296]{0:T(1024)}, f32[311296]{0:T(1024)S(1)}, /*index=5*/f32[311296]{0:T(1024)S(1)}) fusion(f32[311296]{0:T(1024)} %scatter_custom_fusion, f32[]{:T(128)} %bitcast.53, f32[]{:T(128)} %bitcast.48, f32[]{:T(128)} %bitcast.43, f32[]{:T(128)} %bitcast.38, ...), kind=kLoop, calls=%fused_computation.423 | loop fusion | flops 1867776 | bytes 8716312 | tf_op jit(solution)/shard_map/mul | solution.py:125
  69.6 2.0 slice.966
  71.6 1.8 reshape.673
  75.2 1.8 reshape.670
  78.7 5.9 %pad_maximum_fusion = (f32[4,16,152,128]{3,2,1,0:T(8,128)S(1)}, f32[4,16,152,128]{3,2,1,0:T(8,128)}) fusion(f32[4,16,12,128]{3,2,1,0:T(8,128)} %reshape.673, f32[4,16,128,128]{3,2,1,0:T(8,128)} %bitcast.475, f32[4,16,12,128]{3,2,1,0:T(8,128)} %reshape.670, f32[4,16,12,128]{3,2,1,0:T(8,128)S(1)} %reshape.687, f32[4,16,128,128]{3,2,1,0:T(8,128)} %bitcast.477, ...), kind=kLoop, calls=%fused_computation.14 | loop fusion | flops 4980736 | bytes 19922944 | tf_op jit(solution)/shard_map/concatenate | solution.py:93
  87.5 2.2 collective-permute-done.4
  93.2 2.3 pad_maximum_fusion.2
  99.4 5.0 %add_multiply_fusion.10 = (f32[16,152,128]{2,1,0:T(8,128)}, f32[16,152,128]{2,1,0:T(8,128)}, f32[16,152,128]{2,1,0:T(8,128)S(1)}, f32[16,152,128]{2,1,0:T(8,128)S(1)}, f32[16,152,128]{2,1,0:T(8,128)S(1)}) fusion(f32[4,16,152,128]{3,2,1,0:T(8,128)} %get-tuple-element.112, f32[3,16,152,128]{3,2,1,0:T(8,128)S(1)} %pad_maximum_fusion.2, ...), kind=kLoop, calls=%fused_computation.368 | loop fusion | flops 12451840 | bytes 18677760 | tf_op jit(solution)/shard_map/mul | solution.py:146
  105.9 2.3 add_add_fusion.7
  110.5 3.0 add_add_fusion.5
  114.8 6.5 %add_add_fusion.3 = (f32[16,152,128]{2,1,0:T(8,128)}, f32[16,152,128]{2,1,0:T(8,128)}, f32[16,152,128]{2,1,0:T(8,128)}) fusion(f32[16,152,128]{2,1,0:T(8,128)S(1)} %bitcast.460, f32[16,152,128]{2,1,0:T(8,128)S(1)} %get-tuple-element.36, f32[16,152,128]{2,1,0:T(8,128)S(1)} %bitcast.442, f32[16,152,128]{2,1,0:T(8,128)S(1)} %get-tuple-element.35, ...), kind=kLoop, calls=%fused_computation.377 | loop fusion | flops 12451840 | bytes 16187392 | tf_op jit(solution)/shard_map/add | solution.py:127
  121.3 4.4 %add_add_fusion.4 = f32[16,152,128]{2,1,0:T(8,128)} fusion(f32[16,152,128]{2,1,0:T(8,128)} %bitcast.456, f32[16,152,128]{2,1,0:T(8,128)} %get-tuple-element.32, f32[16,152,128]{2,1,0:T(8,128)} %get-tuple-element.31, f32[3,16,152,128]{3,2,1,0:T(8,128)S(1)} %pad_maximum_fusion.2, f32[16,152,128]{2,1,0:T(8,128)S(1)} %bitcast.443, ...), kind=kLoop, calls=%fused_computation.380 | loop fusion | flops 7471104 | bytes 18677760 | tf_op jit(solution)/shard_map/add | solution.py:126
  125.7 13.1 %add_add_fusion.1 = (f32[16,152,128]{2,1,0:T(8,128)}, f32[16,152,128]{2,1,0:T(8,128)}, f32[16,152,128]{2,1,0:T(8,128)}) fusion(f32[16,152,128]{2,1,0:T(8,128)} %bitcast.461, f32[16,152,128]{2,1,0:T(8,128)} %bitcast.457, f32[16,152,128]{2,1,0:T(8,128)} %get-tuple-element.32, f32[16,152,128]{2,1,0:T(8,128)} %get-tuple-element.31, ...), kind=kLoop, calls=%fused_computation.373 | loop fusion | flops 14630912 | bytes 19922944 | tf_op jit(solution)/shard_map/add | solution.py:127
  138.8 6.9 %add_add_fusion.2 = f32[16,152,128]{2,1,0:T(8,128)} fusion(f32[16,152,128]{2,1,0:T(8,128)} %bitcast.462, f32[16,152,128]{2,1,0:T(8,128)} %get-tuple-element.29, f32[16,152,128]{2,1,0:T(8,128)} %get-tuple-element.28, f32[3,16,152,128]{3,2,1,0:T(8,128)S(1)} %pad_maximum_fusion.2, f32[16,152,128]{2,1,0:T(8,128)} %bitcast.458, ...), kind=kLoop, calls=%fused_computation.376 | loop fusion | flops 9961472 | bytes 22413312 | tf_op jit(solution)/shard_map/add | solution.py:126
  145.7 15.8 %add_add_fusion = (f32[16,152,128]{2,1,0:T(8,128)}, f32[16,152,128]{2,1,0:T(8,128)}, f32[16,152,128]{2,1,0:T(8,128)}) fusion(f32[16,152,128]{2,1,0:T(8,128)} %bitcast.466, f32[16,152,128]{2,1,0:T(8,128)} %bitcast.463, f32[16,152,128]{2,1,0:T(8,128)} %get-tuple-element.29, f32[16,152,128]{2,1,0:T(8,128)} %get-tuple-element.28, ...), kind=kLoop, calls=%fused_computation.372 | loop fusion | flops 20545536 | bytes 28639232 | tf_op jit(solution)/shard_map/add | solution.py:126
  161.5 2.1 gather_fusion.6
  163.6 2.0 gather_fusion.4
  165.6 2.0 gather_fusion.3
  167.6 2.0 gather_fusion.2
  169.6 2.0 gather_fusion.1
  171.6 2.0 gather_fusion.5
  174.9 5.0 %collective-permute-start.5 = (f32[7,128]{1,0:T(8,128)S(1)}, f32[7,128]{1,0:T(8,128)S(1)}, u32[]{:S(2)}, u32[]{:S(2)}) collective-permute-start(f32[7,128]{1,0:T(8,128)S(1)} %concatenate.93), channel_id=1, source_target_pairs={{0,1},{1,2},{2,3},{3,4},{4,5},{5,6},{6,7},{8,9},{9,10},{10,11},{11... | collective-permute-start | bytes 10760 | tf_op jit(solution)/shard_map/ppermute | solution.py:52
  181.3 4.4 %scatter_custom_fusion.1 = f32[311296]{0:T(1024)} fusion(s32[384]{0:T(512)S(1)} %fusion.260, f32[384]{0:T(512)S(1)} %pad_maximum_fusion.6, f32[]{:T(128)} %constant.242.clone.1), kind=kCustom, calls=%fused_computation.440 | custom fusion | flops 384 | bytes 1245188 | tf_op jit(solution)/shard_map/scatter-add | solution.py:151
  185.7 4.3 %scatter_custom_fusion.2 = f32[311296]{0:T(1024)} fusion(s32[384]{0:T(512)S(1)} %fusion.260, f32[384]{0:T(512)S(1)} %pad_maximum_fusion.7, f32[]{:T(128)} %constant.242.clone.1), kind=kCustom, calls=%fused_computation.438 | custom fusion | flops 384 | bytes 1245188 | tf_op jit(solution)/shard_map/scatter-add | solution.py:151
  190.0 4.4 %scatter_custom_fusion.3 = f32[311296]{0:T(1024)} fusion(s32[384]{0:T(512)S(1)} %fusion.260, f32[384]{0:T(512)S(1)} %pad_maximum_fusion.8, f32[]{:T(128)} %constant.242.clone.1), kind=kCustom, calls=%fused_computation.436 | custom fusion | flops 384 | bytes 1245188 | tf_op jit(solution)/shard_map/scatter-add | solution.py:151
  194.4 4.4 %scatter_custom_fusion.4 = f32[311296]{0:T(1024)} fusion(s32[384]{0:T(512)S(1)} %fusion.260, f32[384]{0:T(512)S(1)} %pad_maximum_fusion.9, f32[]{:T(128)} %constant.242.clone.1), kind=kCustom, calls=%fused_computation.434 | custom fusion | flops 384 | bytes 1245188 | tf_op jit(solution)/shard_map/scatter-add | solution.py:151
  198.8 4.6 %scatter_custom_fusion.5 = f32[311296]{0:T(1024)} fusion(s32[384]{0:T(512)S(1)} %fusion.260, f32[384]{0:T(512)S(1)} %pad_maximum_fusion.10, f32[]{:T(128)} %constant.242.clone.1), kind=kCustom, calls=%fused_computation.432 | custom fusion | flops 384 | bytes 1245188 | tf_op jit(solution)/shard_map/scatter-add | solution.py:151
  203.4 11.5 %add_multiply_fusion.9 = (f32[16,152,128]{2,1,0:T(8,128)S(1)}, f32[16,152,128]{2,1,0:T(8,128)S(1)}, f32[16,152,128]{2,1,0:T(8,128)S(1)}) fusion(f32[3,16,152,128]{3,2,1,0:T(8,128)} %copy-done, f32[4,16,152,128]{3,2,1,0:T(8,128)} %get-tuple-element.112, f32[16,152,128]{2,1,0:T(8,128)} %get-tuple-element.43, f32[16,152,128]{2,1,0:T(8,128)} %bitcast.483, ...), kind=kLoop, calls=%fused_computation.367 | loop fusion | flops 11517952 | bytes 16187392 | tf_op jit(solution)/shard_map/mul | solution.py:145
  215.2 1.9 copy-done.49
  217.1 3.7 %add_multiply_fusion.7 = (f32[16,152,128]{2,1,0:T(8,128)S(1)}, f32[16,152,128]{2,1,0:T(8,128)S(1)}, f32[16,152,128]{2,1,0:T(8,128)S(1)}) fusion(f32[3,16,152,128]{3,2,1,0:T(8,128)S(1)} %copy-done.1, f32[4,16,152,128]{3,2,1,0:T(8,128)} %get-tuple-element.112, f32[16,152,128]{2,1,0:T(8,128)S(1)} %get-tuple-element.21, f32[16,152,128]{2,1,0:T(8,128)S(1)} %bitcast.482, ...), kind=kLoop, calls=%fused_computation.363 | loop fusion | flops 11517952 | bytes 16187392 | tf_op jit(solution)/shard_map/mul | solution.py:145
  221.1 1.9 copy-done.48
  223.1 2.4 add_multiply_fusion.5
  225.7 1.9 copy-done.47
  227.7 2.4 add_multiply_fusion.3
  232.3 3.4 %add_multiply_fusion.1 = (f32[16,152,128]{2,1,0:T(8,128)S(1)}, f32[16,152,128]{2,1,0:T(8,128)}, f32[16,152,128]{2,1,0:T(8,128)}) fusion(f32[3,16,152,128]{3,2,1,0:T(8,128)S(1)} %copy-done.1, f32[16,152,128]{2,1,0:T(8,128)S(1)} %get-tuple-element.16, f32[16,152,128]{2,1,0:T(8,128)S(1)} %get-tuple-element.12, f32[16,152,128]{2,1,0:T(8,128)S(1)} %bitcast.479, ...), kind=kLoop, calls=%fused_computation.351 | loop fusion | flops 11517952 | bytes 16187392 | tf_op jit(solution)/shard_map/mul | solution.py:145
  235.7 4.2 %add_subtract_fusion = (f32[16,152,128]{2,1,0:T(8,128)}, f32[16,152,128]{2,1,0:T(8,128)}, f32[16,152,128]{2,1,0:T(8,128)}, f32[16,152,128]{2,1,0:T(8,128)}, f32[16,152,128]{2,1,0:T(8,128)}, /*index=5*/f32[16,152,128]{2,1,0:T(8,128)}) fusion(f32[16,152,128]{2,1,0:T(8,128)S(1)} %get-tuple-element.7), kind=kLoop, calls=%fused_computation.350 | loop fusion | flops 3424256 | bytes 8716288 | tf_op jit(solution)/shard_map/sub | solution.py:37
  239.9 4.7 %scatter_custom_fusion.6 = f32[311296]{0:T(1024)} fusion(s32[384]{0:T(512)S(1)} %fusion.260, f32[384]{0:T(512)S(1)} %pad_maximum_fusion.11, f32[]{:T(128)} %constant.242.clone.1), kind=kCustom, calls=%fused_computation.430 | custom fusion | flops 384 | bytes 1245188 | tf_op jit(solution)/shard_map/scatter-add | solution.py:151
  244.6 3.9 %broadcast_multiply_fusion.6 = (f32[16,152,128]{2,1,0:T(8,128)}, f32[16,152,128]{2,1,0:T(8,128)S(1)}) fusion(f32[16,152,128]{2,1,0:T(8,128)} %get-tuple-element.9, f32[16,152,128]{2,1,0:T(8,128)} %get-tuple-element.8, f32[3,16,152,128]{3,2,1,0:T(8,128)} %copy-done), kind=kLoop, calls=%fused_computation.429 | loop fusion | flops 1245184 | bytes 7471104 | tf_op jit(solution)/shard_map/mul | solution.py:37
  248.5 2.0 fusion.99
  252.7 5.2 %multiply_add_fusion.2 = (f32[16,128,128]{2,1,0:T(8,128)}, f32[16,128,128]{2,1,0:T(8,128)S(1)}) fusion(f32[16,152,128]{2,1,0:T(8,128)S(1)} %copy-done.37, f32[16,152,128]{2,1,0:T(8,128)S(1)} %copy-done.7, f32[16,152,128]{2,1,0:T(8,128)S(1)} %get-tuple-element.34, f32[16,152,128]{2,1,0:T(8,128)S(1)} %copy-done.12, f32[16,152,128]{2,1,0:T(8,128)S(1)} %copy-done.25, ...), kind=kLoop, calls=%fused_computation.421 | loop fusion | flops 5505024 | bytes 20971520 | tf_op jit(solution)/shard_map/add | solution.py:159
  259.2 6.5 %multiply_add_fusion.1 = (f32[16,128,128]{2,1,0:T(8,128)}, f32[16,128,128]{2,1,0:T(8,128)}) fusion(f32[16,128,128]{2,1,0:T(8,128)S(1)} %get-tuple-element.4, f32[16,152,128]{2,1,0:T(8,128)S(1)} %copy-done.35, f32[16,152,128]{2,1,0:T(8,128)S(1)} %copy-done.5, f32[16,152,128]{2,1,0:T(8,128)S(1)} %get-tuple-element.35, f32[16,152,128]{2,1,0:T(8,128)S(1)} %copy-done.19, ...), kind=kLoop, calls=%fused_computation.420 | loop fusion | flops 8126464 | bytes 30408704 | tf_op jit(solution)/shard_map/add | solution.py:160
  265.7 5.0 %fusion.232 = (f32[1,16,128,128]{3,2,1,0:T(8,128)S(1)}, f32[16,128,128]{2,1,0:T(8,128)S(1)}) fusion(f32[16,152,128]{2,1,0:T(8,128)} %bitcast.467, f32[16,152,128]{2,1,0:T(8,128)} %get-tuple-element.51, f32[16,152,128]{2,1,0:T(8,128)} %get-tuple-element.30, f32[16,152,128]{2,1,0:T(8,128)} %get-tuple-element.27, f32[16,152,128]{2,1,0:T(8,128)} %get-tuple-element.50, ...), kind=kLoop, calls=%fused_computation.395 | loop fusion | flops 4718592 | bytes 20971520 | tf_op jit(solution)/shard_map/stack | solution.py:170
  270.8 2.0 maximum_bitcast_fusion
  277.2 36.0 %reduce-scatter.2.cloned.1.call-done = f32[1,3,4,128,128]{4,3,2,1,0:T(8,128)} async-done(((f32[4,3,4,128,128]{4,3,2,1,0:T(8,128)}), f32[1,3,4,128,128]{4,3,2,1,0:T(8,128)}) %reduce-scatter.2.cloned.1.call-update) | async-done | bytes 786448 | tf_op jit(solution)/shard_map/reduce_scatter | solution.py:166
  (203 shorter events, 49.2 us)
Async XLA Ops:
  7.2 86.1 %all-gather.2.cloned.1.call-start = ((), (), s32[]{:S(2)}) async-start(), calls=%async_computation.1 | async-start | bytes 3932160 | tf_op jit(solution)/shard_map/all_gather | solution.py:67
  7.9 305.3 %reduce-scatter.2.cloned.1.call-start = ((), (), s32[]{:S(2)}) async-start(), calls=%async_computation.2 | async-start | bytes 3932160 | tf_op jit(solution)/shard_map/reduce_scatter | solution.py:166
  11.3 42.8 %collective-permute-start.1 = (f32[913,128]{1,0:T(8,128)S(1)}, f32[913,128]{1,0:T(8,128)}, u32[]{:S(2)}, u32[]{:S(2)}) collective-permute-start(f32[913,128]{1,0:T(8,128)S(1)} %get-tuple-element.92), channel_id=1, source_target_pairs={{1,0},{2,1},{3,2},{4,3},{5,4},{6,5},{7,6},{9,8},{10,9},{11,10},{12... | collective-permute-start | bytes 1402376 | tf_op jit(solution)/shard_map/ppermute | solution.py:53
  12.6 43.4 %collective-permute-start = (f32[913,128]{1,0:T(8,128)S(1)}, f32[913,128]{1,0:T(8,128)}, u32[]{:S(2)}, u32[]{:S(2)}) collective-permute-start(f32[913,128]{1,0:T(8,128)S(1)} %get-tuple-element.91), channel_id=1, source_target_pairs={{0,1},{1,2},{2,3},{3,4},{4,5},{5,6},{6,7},{8,9},{9,10},{10,11},{11... | collective-permute-start | bytes 1402376 | tf_op jit(solution)/shard_map/ppermute | solution.py:52
  20.3 6.1 %copy-start.59 = (s32[1,128]{1,0:T(1,128)S(1)}, s32[1,128]{1,0:T(1,128)}, u32[]{:S(2)}) copy-start(s32[1,128]{1,0:T(1,128)} %param.12) | copy-start | bytes 1540
  20.3 6.3 %copy-start.57 = (f32[1,6]{1,0:T(1,128)S(1)}, f32[1,6]{1,0:T(1,128)}, u32[]{:S(2)}) copy-start(f32[1,6]{1,0:T(1,128)} %param.11) | copy-start | bytes 76
  20.3 15.0 %collective-permute-start.8 = (f32[768,128]{1,0:T(8,128)S(1)}, f32[768,128]{1,0:T(8,128)S(1)}, u32[]{:S(2)}, u32[]{:S(2)}) collective-permute-start(f32[768,128]{1,0:T(8,128)S(1)} %reshape.686), channel_id=1, source_target_pairs={{1,0},{2,1},{3,2},{4,3},{5,4},{6,5},{7,6},{9,8},{10,9},{11,10},{12... | collective-permute-start | bytes 1179656 | tf_op jit(solution)/shard_map/ppermute | solution.py:53
  21.7 32.3 %collective-permute-start.7 = (f32[768,128]{1,0:T(8,128)S(1)}, f32[768,128]{1,0:T(8,128)S(1)}, u32[]{:S(2)}, u32[]{:S(2)}) collective-permute-start(f32[768,128]{1,0:T(8,128)S(1)} %reshape.684), channel_id=1, source_target_pairs={{0,1},{1,2},{2,3},{3,4},{4,5},{5,6},{6,7},{8,9},{9,10},{10,11},{11... | collective-permute-start | bytes 1179656 | tf_op jit(solution)/shard_map/ppermute | solution.py:52
  60.5 16.6 %collective-permute-start.2 = (f32[3,4,24,128]{3,2,1,0:T(8,128)}, f32[3,4,24,128]{3,2,1,0:T(8,128)}, u32[]{:S(2)}, u32[]{:S(2)}) collective-permute-start(f32[3,4,24,128]{3,2,1,0:T(8,128)} %pad_maximum_fusion.5), channel_id=1, source_target_pairs={{0,8},{8,16},{16,24},{24,0},{1,9},{9,17},{17,25},{25,1},{2,10},{10... | collective-permute-start | bytes 442376 | tf_op jit(solution)/shard_map/ppermute | solution.py:23
  69.6 38.6 %copy-start.9 = (f32[311296]{0:T(1024)}, f32[311296]{0:T(1024)S(1)}, u32[]{:S(2)}) copy-start(f32[311296]{0:T(1024)S(1)} %get-tuple-element.73) | copy-start | bytes 3735556
  77.1 7.5 %collective-permute-start.3 = (f32[3,4,24,128]{3,2,1,0:T(8,128)}, f32[3,4,24,128]{3,2,1,0:T(8,128)S(1)}, u32[]{:S(2)}, u32[]{:S(2)}) collective-permute-start(f32[3,4,24,128]{3,2,1,0:T(8,128)} %collective-permute-done.2), channel_id=1, source_target_pairs={{0,8},{8,16},{16,24},{24,0},{1,9},{9,17},{17,25},{25,1},{2,10},{10... | collective-permute-start | bytes 442376 | tf_op jit(solution)/shard_map/ppermute | solution.py:23
  84.5 5.1 %collective-permute-start.4 = (f32[3,4,24,128]{3,2,1,0:T(8,128)S(1)}, f32[3,4,24,128]{3,2,1,0:T(8,128)S(1)}, u32[]{:S(2)}, u32[]{:S(2)}) collective-permute-start(f32[3,4,24,128]{3,2,1,0:T(8,128)S(1)} %collective-permute-done.3), channel_id=1, source_target_pairs={{0,8},{8,16},{16,24},{24,0},{1,9},{9,17},{17,25},{25,1},{2,10},{10... | collective-permute-start | bytes 442376 | tf_op jit(solution)/shard_map/ppermute | solution.py:23
  95.6 50.1 %copy-start = (f32[3,16,152,128]{3,2,1,0:T(8,128)}, f32[3,16,152,128]{3,2,1,0:T(8,128)S(1)}, u32[]{:S(2)}) copy-start(f32[3,16,152,128]{3,2,1,0:T(8,128)S(1)} %pad_maximum_fusion.2) | copy-start | bytes 11206660
  104.4 10.0 %copy-start.26 = (f32[16,152,128]{2,1,0:T(8,128)}, f32[16,152,128]{2,1,0:T(8,128)S(1)}, u32[]{:S(2)}) copy-start(f32[16,152,128]{2,1,0:T(8,128)S(1)} %get-tuple-element.52) | copy-start | bytes 3735556
  105.9 15.4 %copy-start.8 = (f32[16,152,128]{2,1,0:T(8,128)}, f32[16,152,128]{2,1,0:T(8,128)S(1)}, u32[]{:S(2)}) copy-start(f32[16,152,128]{2,1,0:T(8,128)S(1)} %fusion.220) | copy-start | bytes 3735556
  108.2 6.2 %copy-start.33 = (f32[16,152,128]{2,1,0:T(8,128)}, f32[16,152,128]{2,1,0:T(8,128)S(1)}, u32[]{:S(2)}) copy-start(f32[16,152,128]{2,1,0:T(8,128)S(1)} %get-tuple-element.36) | copy-start | bytes 3735556
  108.2 37.5 %copy-start.4 = (f32[16,152,128]{2,1,0:T(8,128)}, f32[16,152,128]{2,1,0:T(8,128)S(1)}, u32[]{:S(2)}) copy-start(f32[16,152,128]{2,1,0:T(8,128)S(1)} %get-tuple-element.38) | copy-start | bytes 3735556
  108.2 37.5 %copy-start.6 = (f32[16,152,128]{2,1,0:T(8,128)}, f32[16,152,128]{2,1,0:T(8,128)S(1)}, u32[]{:S(2)}) copy-start(f32[16,152,128]{2,1,0:T(8,128)S(1)} %get-tuple-element.37) | copy-start | bytes 3735556
  108.8 4.7 %copy-start.42 = (f32[16,152,128]{2,1,0:T(8,128)}, f32[16,152,128]{2,1,0:T(8,128)S(1)}, u32[]{:S(2)}) copy-start(f32[16,152,128]{2,1,0:T(8,128)S(1)} %add_add_fusion.8) | copy-start | bytes 3735556
  114.4 6.9 %copy-start.41 = (f32[16,152,128]{2,1,0:T(8,128)}, f32[16,152,128]{2,1,0:T(8,128)S(1)}, u32[]{:S(2)}) copy-start(f32[16,152,128]{2,1,0:T(8,128)S(1)} %add_add_fusion.6) | copy-start | bytes 3735556
  163.6 10.0 %copy-start.58 = (f32[1,6,128]{2,0,1:T(1,128)S(1)}, f32[1,6,128]{2,0,1:T(1,128)}, u32[]{:S(2)}) copy-start(f32[1,6,128]{2,0,1:T(1,128)} %param.13) | copy-start | bytes 9220
  173.6 6.3 %collective-permute-start.6 = (f32[7,128]{1,0:T(8,128)S(1)}, f32[7,128]{1,0:T(8,128)S(1)}, u32[]{:S(2)}, u32[]{:S(2)}) collective-permute-start(f32[7,128]{1,0:T(8,128)S(1)} %concatenate.93), channel_id=1, source_target_pairs={{1,0},{2,1},{3,2},{4,3},{5,4},{6,5},{7,6},{9,8},{10,9},{11,10},{12... | collective-permute-start | bytes 10760 | tf_op jit(solution)/shard_map/ppermute | solution.py:53
  174.9 6.3 %collective-permute-start.5 = (f32[7,128]{1,0:T(8,128)S(1)}, f32[7,128]{1,0:T(8,128)S(1)}, u32[]{:S(2)}, u32[]{:S(2)}) collective-permute-start(f32[7,128]{1,0:T(8,128)S(1)} %concatenate.93), channel_id=1, source_target_pairs={{0,1},{1,2},{2,3},{3,4},{4,5},{5,6},{6,7},{8,9},{9,10},{10,11},{11... | collective-permute-start | bytes 10760 | tf_op jit(solution)/shard_map/ppermute | solution.py:52
  203.4 11.6 %copy-start.1 = (f32[3,16,152,128]{3,2,1,0:T(8,128)S(1)}, f32[3,16,152,128]{3,2,1,0:T(8,128)}, u32[]{:S(2)}) copy-start(f32[3,16,152,128]{3,2,1,0:T(8,128)} %copy-done) | copy-start | bytes 11206660
  214.9 6.2 %copy-start.14 = (f32[16,152,128]{2,1,0:T(8,128)}, f32[16,152,128]{2,1,0:T(8,128)S(1)}, u32[]{:S(2)}) copy-start(f32[16,152,128]{2,1,0:T(8,128)S(1)} %get-tuple-element.23) | copy-start | bytes 3735556
  214.9 6.2 %copy-start.20 = (f32[16,152,128]{2,1,0:T(8,128)}, f32[16,152,128]{2,1,0:T(8,128)S(1)}, u32[]{:S(2)}) copy-start(f32[16,152,128]{2,1,0:T(8,128)S(1)} %get-tuple-element.22) | copy-start | bytes 3735556
  220.8 4.9 %copy-start.16 = (f32[16,152,128]{2,1,0:T(8,128)}, f32[16,152,128]{2,1,0:T(8,128)S(1)}, u32[]{:S(2)}) copy-start(f32[16,152,128]{2,1,0:T(8,128)S(1)} %get-tuple-element.20) | copy-start | bytes 3735556
  220.9 4.9 %copy-start.22 = (f32[16,152,128]{2,1,0:T(8,128)}, f32[16,152,128]{2,1,0:T(8,128)S(1)}, u32[]{:S(2)}) copy-start(f32[16,152,128]{2,1,0:T(8,128)S(1)} %get-tuple-element.19) | copy-start | bytes 3735556
  225.5 4.9 %copy-start.18 = (f32[16,152,128]{2,1,0:T(8,128)}, f32[16,152,128]{2,1,0:T(8,128)S(1)}, u32[]{:S(2)}) copy-start(f32[16,152,128]{2,1,0:T(8,128)S(1)} %get-tuple-element.17) | copy-start | bytes 3735556
  225.5 4.9 %copy-start.24 = (f32[16,152,128]{2,1,0:T(8,128)}, f32[16,152,128]{2,1,0:T(8,128)S(1)}, u32[]{:S(2)}) copy-start(f32[16,152,128]{2,1,0:T(8,128)S(1)} %get-tuple-element.16) | copy-start | bytes 3735556
  244.6 5.9 %copy-start.25 = (f32[16,152,128]{2,1,0:T(8,128)S(1)}, f32[16,152,128]{2,1,0:T(8,128)}, u32[]{:S(2)}) copy-start(f32[16,152,128]{2,1,0:T(8,128)} %copy-done.24) | copy-start | bytes 3735556
  244.6 5.9 %copy-start.28 = (f32[16,152,128]{2,1,0:T(8,128)S(1)}, f32[16,152,128]{2,1,0:T(8,128)}, u32[]{:S(2)}) copy-start(f32[16,152,128]{2,1,0:T(8,128)} %get-tuple-element.28) | copy-start | bytes 3735556
  244.6 5.9 %copy-start.32 = (f32[16,152,128]{2,1,0:T(8,128)S(1)}, f32[16,152,128]{2,1,0:T(8,128)}, u32[]{:S(2)}) copy-start(f32[16,152,128]{2,1,0:T(8,128)} %copy-done.31) | copy-start | bytes 3735556
  244.6 5.9 %copy-start.37 = (f32[16,152,128]{2,1,0:T(8,128)S(1)}, f32[16,152,128]{2,1,0:T(8,128)}, u32[]{:S(2)}) copy-start(f32[16,152,128]{2,1,0:T(8,128)} %copy-done.36) | copy-start | bytes 3735556
  244.6 5.9 %copy-start.38 = (f32[16,152,128]{2,1,0:T(8,128)S(1)}, f32[16,152,128]{2,1,0:T(8,128)}, u32[]{:S(2)}) copy-start(f32[16,152,128]{2,1,0:T(8,128)} %get-tuple-element.8) | copy-start | bytes 3735556
  244.6 5.9 %copy-start.39 = (f32[16,152,128]{2,1,0:T(8,128)S(1)}, f32[16,152,128]{2,1,0:T(8,128)}, u32[]{:S(2)}) copy-start(f32[16,152,128]{2,1,0:T(8,128)} %get-tuple-element.25) | copy-start | bytes 3735556
  248.5 4.1 %copy-start.23 = (f32[16,152,128]{2,1,0:T(8,128)S(1)}, f32[16,152,128]{2,1,0:T(8,128)}, u32[]{:S(2)}) copy-start(f32[16,152,128]{2,1,0:T(8,128)} %copy-done.22) | copy-start | bytes 3735556
  252.6 5.3 %copy-start.5 = (f32[16,152,128]{2,1,0:T(8,128)S(1)}, f32[16,152,128]{2,1,0:T(8,128)}, u32[]{:S(2)}) copy-start(f32[16,152,128]{2,1,0:T(8,128)} %copy-done.4) | copy-start | bytes 3735556
  252.6 5.3 %copy-start.11 = (f32[16,152,128]{2,1,0:T(8,128)S(1)}, f32[16,152,128]{2,1,0:T(8,128)}, u32[]{:S(2)}) copy-start(f32[16,152,128]{2,1,0:T(8,128)} %get-tuple-element.32) | copy-start | bytes 3735556
  252.6 5.3 %copy-start.15 = (f32[16,152,128]{2,1,0:T(8,128)S(1)}, f32[16,152,128]{2,1,0:T(8,128)}, u32[]{:S(2)}) copy-start(f32[16,152,128]{2,1,0:T(8,128)} %copy-done.14) | copy-start | bytes 3735556
  252.6 5.3 %copy-start.17 = (f32[16,152,128]{2,1,0:T(8,128)S(1)}, f32[16,152,128]{2,1,0:T(8,128)}, u32[]{:S(2)}) copy-start(f32[16,152,128]{2,1,0:T(8,128)} %copy-done.16) | copy-start | bytes 3735556
  252.6 5.3 %copy-start.19 = (f32[16,152,128]{2,1,0:T(8,128)S(1)}, f32[16,152,128]{2,1,0:T(8,128)}, u32[]{:S(2)}) copy-start(f32[16,152,128]{2,1,0:T(8,128)} %copy-done.18) | copy-start | bytes 3735556
  252.6 5.8 %copy-start.27 = (f32[16,152,128]{2,1,0:T(8,128)S(1)}, f32[16,152,128]{2,1,0:T(8,128)}, u32[]{:S(2)}) copy-start(f32[16,152,128]{2,1,0:T(8,128)} %get-tuple-element.29) | copy-start | bytes 3735556
  252.7 6.2 %copy-start.30 = (f32[16,152,128]{2,1,0:T(8,128)S(1)}, f32[16,152,128]{2,1,0:T(8,128)}, u32[]{:S(2)}) copy-start(f32[16,152,128]{2,1,0:T(8,128)} %copy-done.29) | copy-start | bytes 3735556
  252.7 6.5 %copy-start.35 = (f32[16,152,128]{2,1,0:T(8,128)S(1)}, f32[16,152,128]{2,1,0:T(8,128)}, u32[]{:S(2)}) copy-start(f32[16,152,128]{2,1,0:T(8,128)} %copy-done.34) | copy-start | bytes 3735556
  265.7 5.1 %copy-start.50 = (f32[16,128,128]{2,1,0:T(8,128)S(1)}, f32[16,128,128]{2,1,0:T(8,128)}, u32[]{:S(2)}) copy-start(f32[16,128,128]{2,1,0:T(8,128)} %get-tuple-element.3) | copy-start | bytes 3145732
  265.7 5.1 %copy-start.51 = (f32[16,128,128]{2,1,0:T(8,128)S(1)}, f32[16,128,128]{2,1,0:T(8,128)}, u32[]{:S(2)}) copy-start(f32[16,128,128]{2,1,0:T(8,128)} %get-tuple-element.5) | copy-start | bytes 3145732
  275.7 37.5 %copy-start.52 = (f32[3,4,128,128]{3,2,1,0:T(8,128)S(1)}, f32[3,4,128,128]{3,2,1,0:T(8,128)}, u32[]{:S(2)}) copy-start(f32[3,4,128,128]{3,2,1,0:T(8,128)} %param.7) | copy-start | bytes 2359300
  (25 other events, 61.5 us)
Sparse Core Ops, SparseCore 0:
  9.5 31.2 all-gather.1
  272.9 40.2 reduce-scatter.1
